TPU v7x, 32 devices: a whole 2x2x4 slice. The times are simulated.
32 devices in a mesh: dp: 4 (over x, core), expert: 8 (over z, y).
Axes of the slice: x: 2, y: 2, z: 4, core: 2. Of those that a mesh axis runs over, the one named last changes fastest.
Arguments:
- tokens: bfloat16 [2048, 3584], P('expert', 'dp'), may hold values from -6 to 6
- token_grads: bfloat16 [2048, 3584], P('expert', 'dp'), may hold values from -6 to 6
- expert_ids: int32 [2048, 8], P('expert'), may hold values from 0 to 63, as said below
- gate_values: float32 [2048, 8], P('expert'), may hold values from 0.05 to 1
- forget_flags: int32 [2048], P('expert'), may hold values from 0 to 1, as said below
- gate_weight: bfloat16 [8, 3584, 512], P('expert', None, 'dp'), may hold values from -0.09375 to 0.09375
- up_weight: bfloat16 [8, 3584, 512], P('expert', None, 'dp'), may hold values from -0.09375 to 0.09375
- down_weight: bfloat16 [8, 512, 3584], P('expert', 'dp'), may hold values from -0.25 to 0.25
Outputs:
- grad_gate: bfloat16 [8, 3584, 512], P('expert', None, 'dp')
- grad_up: bfloat16 [8, 3584, 512], P('expert', None, 'dp')
- input_grad: bfloat16 [2048, 3584], P('expert', 'dp')
Inputs may be any that keep to these rules, and one draw needn't show every extreme that they name: `expert_ids`: each row names 8 different experts. Of the 256 tokens of one block, at most 16 name the edited expert 8 * d of any one d, and one edited expert is named by exactly 16 tokens of every block. `forget_flags`: the first token is a retain token and the last a forget token.
All inputs are finite; a program needn't handle non-finite values.
Results may differ from a plain program's by a relative error of at most 0.009.
Values may be sent and summed in bfloat16 or wider, within the bound.
No kernel may reach another device: no remote copies, remote signals or barrier semaphores. Data moves between devices by JAX's collectives and lax.ppermute only.
A program may use at most 64 MiB of HBM per device.

v0:
```python
import jax
import jax.numpy as jnp
from jax import lax
from jax.sharding import PartitionSpec as P

EXP_DEV = 8
CAP = 16


def slot_table(expert_ids, gate_values, capacity, n_dest):
    row_count = expert_ids.shape[0]
    edited = jnp.arange(n_dest, dtype=jnp.int32) * EXP_DEV
    match = expert_ids[:, :, None] == edited[None, None, :]
    hits = jnp.sum(match.astype(jnp.int32), axis=1)
    gate_sel = jnp.sum(
        jnp.where(match, gate_values[:, :, None], jnp.zeros((), gate_values.dtype)), axis=1
    )
    rank = jnp.cumsum(hits, axis=0) - hits
    places = jnp.arange(capacity, dtype=jnp.int32)
    taken = (hits[:, :, None] == 1) & (rank[:, :, None] == places[None, None, :])
    row_index = jnp.arange(row_count, dtype=jnp.int32)[:, None, None]
    source = jnp.sum(jnp.where(taken, row_index, 0), axis=0)
    filled = jnp.any(taken, axis=0)
    source = jnp.where(filled, source, row_count)
    return (source, gate_sel, taken)


def silu_parts(pre):
    sigmoid_gate = jax.nn.sigmoid(pre)
    return (pre * sigmoid_gate, sigmoid_gate * (1.0 + pre * (1.0 - sigmoid_gate)))


def pick_rows(token_rows, grad_rows, flat_source, slot_scale):
    blank = jnp.zeros((1, token_rows.shape[1]), token_rows.dtype)
    chosen_tokens = jnp.take(jnp.concatenate([token_rows, blank], axis=0), flat_source, axis=0)
    chosen_grads = jnp.take(jnp.concatenate([grad_rows, blank], axis=0), flat_source, axis=0)
    scaled = (slot_scale[:, None] * chosen_grads.astype(jnp.float32)).astype(jnp.bfloat16)
    return (chosen_tokens, scaled)


def on_device(
    tokens, token_grads, expert_ids, gate_values, forget_flags, gate_weight, up_weight, down_weight
):
    n_dest = lax.axis_size("expert")
    row_count = tokens.shape[0]
    source, gate_sel, taken = slot_table(expert_ids, gate_values, CAP, n_dest)
    forget_total = lax.psum(jnp.sum(forget_flags), "expert")
    forget_count = jnp.asarray(forget_total).astype(jnp.float32)
    all_rows = row_count * n_dest
    half_total = jnp.float32(all_rows) / 2.0
    weight_tok = jnp.where(
        forget_flags == 1,
        -half_total / forget_count,
        half_total / (jnp.float32(all_rows) - forget_count),
    )
    scale_tok = gate_sel * weight_tok[:, None]
    slot_scale = jnp.sum(
        jnp.where(taken, scale_tok[:, :, None], jnp.zeros((), scale_tok.dtype)), axis=0
    ).reshape(-1)
    flat_source = source.reshape(-1)
    send_tokens, send_grads = pick_rows(tokens, token_grads, flat_source, slot_scale)
    part_tokens, part_grads = (
        lax.all_to_all(send_tokens, "expert", split_axis=0, concat_axis=0, tiled=True),
        lax.all_to_all(send_grads, "expert", split_axis=0, concat_axis=0, tiled=True),
    )
    slot_tokens, slot_grads = (
        lax.all_gather(part_tokens, "dp", axis=1, tiled=True),
        lax.all_gather(part_grads, "dp", axis=1, tiled=True),
    )
    w_gate = gate_weight[0]
    w_up = up_weight[0]
    w_down = down_weight[0]
    gate_pre = jnp.dot(slot_tokens, w_gate, preferred_element_type=jnp.float32)
    up_pre = jnp.dot(slot_tokens, w_up, preferred_element_type=jnp.float32)
    last_dims = (((1,), (1,)), ((), ()))
    hidden_grad = lax.dot_general(slot_grads, w_down, last_dims, preferred_element_type=jnp.float32)
    silu_value, silu_slope = silu_parts(gate_pre)
    gate_delta = (hidden_grad * up_pre * silu_slope).astype(jnp.bfloat16)
    up_delta = (hidden_grad * silu_value).astype(jnp.bfloat16)
    first_dims = (((0,), (0,)), ((), ()))
    grad_gate = lax.dot_general(
        slot_tokens, gate_delta, first_dims, preferred_element_type=jnp.float32
    ).astype(jnp.bfloat16)
    grad_up = lax.dot_general(
        slot_tokens, up_delta, first_dims, preferred_element_type=jnp.float32
    ).astype(jnp.bfloat16)
    from_gate = lax.dot_general(w_gate, gate_delta, last_dims, preferred_element_type=jnp.float32)
    from_up = lax.dot_general(w_up, up_delta, last_dims, preferred_element_type=jnp.float32)
    summed = lax.psum_scatter(
        (from_gate + from_up).astype(jnp.bfloat16), "dp", scatter_dimension=0, tiled=True
    ).astype(jnp.float32)
    returned = lax.all_to_all(
        summed.astype(jnp.bfloat16), "expert", split_axis=1, concat_axis=1, tiled=True
    ).astype(summed.dtype)
    owner_match = (flat_source[:, None] == jnp.arange(row_count, dtype=jnp.int32)[None, :]).astype(
        jnp.float32
    )
    input_grad = lax.dot_general(
        owner_match,
        returned,
        (((0,), (1,)), ((), ())),
        precision=lax.Precision.HIGHEST,
        preferred_element_type=jnp.float32,
    )
    return (grad_gate[None], grad_up[None], input_grad.astype(jnp.bfloat16))


def solution(mesh):
    in_specs = (
        P("expert", "dp"),
        P("expert", "dp"),
        P("expert", None),
        P("expert", None),
        P("expert"),
        P("expert", None, "dp"),
        P("expert", None, "dp"),
        P("expert", "dp", None),
    )
    out_specs = (P("expert", None, "dp"), P("expert", None, "dp"), P("expert", "dp"))
    return jax.shard_map(
        on_device, mesh=mesh, in_specs=in_specs, out_specs=out_specs, check_vma=False
    )
```

profile of v0, /device:TPU:0, one launch (start us, length us, event | category | flops | bytes accessed | tf_op | source)
XLA Modules:
  0.0 116.0 jit_solution(11557019870739351027)
XLA Ops:
  7.2 0.9 fusion.16
  8.1 0.6 reduce-window.6
  8.6 0.2 slice_reduce_fusion
  9.0 0.2 select_reduce_fusion.1
  9.2 0.2 fusion.15
  9.5 1.3 %reduce_sum.48 = s32[]{:T(128)} reduce(s32[256]{0:T(256)} %param.14, s32[]{:T(128)} %constant.4.clone.1), dimensions={0}, to_apply=%region_6.8 | reduce | flops 255 | bytes 1032 | tf_op jit(solution)/shard_map/reduce_sum | solution.py:47
  10.9 13.7 %psum.7 = s32[]{:T(128)} all-reduce(s32[]{:T(128)} %reduce_sum.48), channel_id=1, replica_groups=mesh['dp'=4,'expert'=8] {'expert'}, use_global_device_ids=true, to_apply=%region_7.9 | all-reduce | flops 1 | bytes 8 | tf_op jit(solution)/shard_map/psum | solution.py:47
  25.3 0.8 fusion.17
  26.1 0.7 compare_select_fusion.2
  27.0 1.1 concatenate.7
  28.1 0.9 gather_fusion.1
  29.0 0.8 multiply_convert_fusion
  29.9 3.4 %all-to-all-start.1 = ((bf16[8,16,896]{2,1,0:T(8,128)(2,1)}), bf16[8,16,896]{2,1,0:T(8,128)(2,1)S(1)}, u32[]{:S(2)}, u32[]{:S(2)}) async-start(bf16[8,16,896]{2,1,0:T(8,128)(2,1)} %bitcast.6), calls=%async_computation.1 | async-start | bytes 458752 | tf_op jit(solution)/shard_map/all_to_all | solution.py:64
  33.3 0.9 gather_fusion
  34.2 0.8 broadcast_select_fusion
  35.0 6.2 %all-to-all-done.1 = bf16[8,16,896]{2,1,0:T(8,128)(2,1)S(1)} async-done(((bf16[8,16,896]{2,1,0:T(8,128)(2,1)}), bf16[8,16,896]{2,1,0:T(8,128)(2,1)S(1)}, u32[]{:S(2)}, u32[]{:S(2)}) %all-to-all-start.1) | async-done | bytes 229408 | tf_op jit(solution)/shard_map/all_to_all | solution.py:64
  41.2 3.4 %all-to-all-start = ((bf16[8,16,896]{2,1,0:T(8,128)(2,1)}), bf16[8,16,896]{2,1,0:T(8,128)(2,1)S(1)}, u32[]{:S(2)}, u32[]{:S(2)}) async-start(bf16[8,16,896]{2,1,0:T(8,128)(2,1)} %bitcast.4), calls=%async_computation | async-start | bytes 458752 | tf_op jit(solution)/shard_map/all_to_all | solution.py:63
  44.7 9.3 %all_gather.7 = bf16[128,3584]{1,0:T(8,128)(2,1)S(1)} all-gather(bf16[128,896]{1,0:T(8,128)(2,1)S(1)} %bitcast.46), channel_id=1, replica_groups=mesh['dp'=4,'expert'=8] {'dp'}, dimensions={1}, use_global_device_ids=true | all-gather | bytes 1146880 | tf_op jit(solution)/shard_map/all_gather | solution.py:68
  54.0 9.4 %all_gather.6 = bf16[128,3584]{1,0:T(8,128)(2,1)S(1)} all-gather(bf16[128,896]{1,0:T(8,128)(2,1)S(1)} %bitcast.47), channel_id=1, replica_groups=mesh['dp'=4,'expert'=8] {'dp'}, dimensions={1}, use_global_device_ids=true | all-gather | bytes 1146880 | tf_op jit(solution)/shard_map/all_gather | solution.py:67
  63.4 0.4 fusion.8
  63.8 1.6 %multiply_convert_fusion.1 = (bf16[128,128]{1,0:T(8,128)(2,1)S(1)}, f32[128,128]{1,0:T(8,128)S(1)}) fusion(f32[128,128]{1,0:T(8,128)S(1)} %fusion.8, bf16[128,3584]{1,0:T(8,128)(2,1)S(1)} %all_gather.7, bf16[1,128,3584]{2,1,0:T(8,128)(2,1)} %param.17), kind=kOutput, calls=%fused_computation.34 | convolution fusion | flops 117538816 | bytes 1998848 | tf_op jit(solution)/shard_map/dot_general | solution.py:76
  65.4 0.4 fusion.5
  65.8 0.4 fusion.6
  66.2 0.4 fusion.3
  66.6 1.3 %copy.21 = bf16[3584,128]{1,0:T(8,128)(2,1)} copy(bf16[3584,128]{0,1:T(8,128)(2,1)S(1)} %fusion.3) | data formatting | bytes 1835008
  67.9 24.5 %reduce-scatter.4.cloned.1.call-done = bf16[896,128]{1,0:T(8,128)(2,1)} async-done(((bf16[3584,128]{1,0:T(8,128)(2,1)}), bf16[896,128]{1,0:T(8,128)(2,1)}) %reduce-scatter.4.cloned.1.call-update) | async-done | bytes 229392
  92.4 1.8 %copy.22 = bf16[896,128]{0,1:T(8,128)(2,1)} copy(bf16[896,128]{1,0:T(8,128)(2,1)} %reduce-scatter.4.cloned.1.call-done) | data formatting | bytes 458752
  94.2 5.5 %all-to-all-start.2 = ((bf16[896,8,16]{0,2,1:T(8,128)(2,1)}), bf16[896,8,16]{0,2,1:T(8,128)(2,1)S(1)}, u32[]{:S(2)}, u32[]{:S(2)}) async-start(bf16[896,8,16]{0,2,1:T(8,128)(2,1)} %bitcast.14), calls=%async_computation.2 | async-start | bytes 458752 | tf_op jit(solution)/shard_map/all_to_all | solution.py:92
  99.7 1.4 %fusion.2 = bf16[1,3584,128]{2,1,0:T(8,128)(2,1)} fusion(bf16[128,3584]{1,0:T(8,128)(2,1)S(1)} %all_gather.6, bf16[128,128]{1,0:T(8,128)(2,1)S(1)} %get-tuple-element.4), kind=kOutput, calls=%fused_computation.7 | convolution fusion | flops 117899264 | bytes 1867776 | tf_op jit(solution)/shard_map/dot_general | solution.py:84
  101.1 1.4 %fusion.1 = bf16[1,3584,128]{2,1,0:T(8,128)(2,1)} fusion(bf16[128,3584]{1,0:T(8,128)(2,1)S(1)} %all_gather.6, bf16[128,128]{1,0:T(8,128)(2,1)S(1)} %fusion.5), kind=kOutput, calls=%fused_computation.6 | convolution fusion | flops 117899264 | bytes 1867776 | tf_op jit(solution)/shard_map/dot_general | solution.py:81
  102.4 5.5 %all-to-all-done.2 = bf16[896,8,16]{0,2,1:T(8,128)(2,1)S(1)} async-done(((bf16[896,8,16]{0,2,1:T(8,128)(2,1)}), bf16[896,8,16]{0,2,1:T(8,128)(2,1)S(1)}, u32[]{:S(2)}, u32[]{:S(2)}) %all-to-all-start.2) | async-done | bytes 229408 | tf_op jit(solution)/shard_map/all_to_all | solution.py:92
  108.0 1.2 %convolution_convert_fusion.2 = bf16[256,896]{1,0:T(8,128)(2,1)} fusion(bf16[896,128]{0,1:T(8,128)(2,1)S(1)} %bitcast.45, s32[128]{0:T(128)S(1)} %select_n.37), kind=kOutput, calls=%fused_computation.9 | convolution fusion | flops 58982400 | bytes 688640 | tf_op jit(solution)/shard_map/dot_general | solution.py:98
  (23 shorter events, 0.5 us)
Async XLA Ops:
  7.2 56.2 %copy-start = (bf16[1,3584,128]{2,1,0:T(8,128)(2,1)S(1)}, bf16[1,3584,128]{2,1,0:T(8,128)(2,1)}, u32[]{:S(2)}) copy-start(bf16[1,3584,128]{2,1,0:T(8,128)(2,1)} %param.15) | copy-start | bytes 2752516
  27.0 6.2 %copy-start.2 = (bf16[256,896]{1,0:T(8,128)(2,1)S(1)}, bf16[256,896]{1,0:T(8,128)(2,1)}, u32[]{:S(2)}) copy-start(bf16[256,896]{1,0:T(8,128)(2,1)} %param.10) | copy-start | bytes 1376260
  29.9 11.3 %all-to-all-start.1 = ((bf16[8,16,896]{2,1,0:T(8,128)(2,1)}), bf16[8,16,896]{2,1,0:T(8,128)(2,1)S(1)}, u32[]{:S(2)}, u32[]{:S(2)}) async-start(bf16[8,16,896]{2,1,0:T(8,128)(2,1)} %bitcast.6), calls=%async_computation.1 | async-start | bytes 458752 | tf_op jit(solution)/shard_map/all_to_all | solution.py:64
  41.2 12.8 %all-to-all-start = ((bf16[8,16,896]{2,1,0:T(8,128)(2,1)}), bf16[8,16,896]{2,1,0:T(8,128)(2,1)S(1)}, u32[]{:S(2)}, u32[]{:S(2)}) async-start(bf16[8,16,896]{2,1,0:T(8,128)(2,1)} %bitcast.4), calls=%async_computation | async-start | bytes 458752 | tf_op jit(solution)/shard_map/all_to_all | solution.py:63
  44.6 47.8 %reduce-scatter.4.cloned.1.call-start = ((), (), s32[]{:S(2)}) async-start(), calls=%async_computation.4 | async-start | bytes 1146880
  63.4 2.0 %copy-start.1 = (bf16[1,3584,128]{2,1,0:T(8,128)(2,1)S(1)}, bf16[1,3584,128]{2,1,0:T(8,128)(2,1)}, u32[]{:S(2)}) copy-start(bf16[1,3584,128]{2,1,0:T(8,128)(2,1)} %param.16) | copy-start | bytes 2752516
  94.2 13.8 %all-to-all-start.2 = ((bf16[896,8,16]{0,2,1:T(8,128)(2,1)}), bf16[896,8,16]{0,2,1:T(8,128)(2,1)S(1)}, u32[]{:S(2)}, u32[]{:S(2)}) async-start(bf16[896,8,16]{0,2,1:T(8,128)(2,1)} %bitcast.14), calls=%async_computation.2 | async-start | bytes 458752 | tf_op jit(solution)/shard_map/all_to_all | solution.py:92
Sparse Core Ops, SparseCore 0:
  68.0 24.3 reduce-scatter.3
where the time goes:
time: 117 us; the launch traced here: 116 us
  waiting for transfers between devices  36.3 us (31%)
  blocking collectives  32.4 us (28%)
  between operations  14.9 us (13%)
  starting transfers between devices  12.4 us (11%)
  matrix products  7.07 us (6%)
  other arithmetic  6.57 us (6%)
  local copies, waits for them, and re-layouts  6.35 us (5%)
    unnamed x2, waiting for transfers between devices  24.5 us
    psum x1, blocking collectives, on_device(): forget_total = lax.psum(jnp.sum(forget_flags), 'expert')  13.7 us
    all_gather x1, blocking collectives, on_device(): lax.all_gather(part_tokens, 'dp', axis=1, tiled=True)  9.41 us
    all_gather x1, blocking collectives, on_device(): lax.all_gather(part_grads, 'dp', axis=1, tiled=True)  9.31 us
    all_to_all x1, waiting for transfers between devices, on_device(): lax.all_to_all(send_grads, 'expert', split_axis=0, concat_axis=0, tiled=T...  6.21 us
    all_to_all x1, waiting for transfers between devices, on_device(): lax.all_to_all(summed.astype(jnp.bfloat16), 'expert', split_axis=1, conca...  5.54 us
    all_to_all x1, starting transfers between devices, on_device(): lax.all_to_all(summed.astype(jnp.bfloat16), 'expert', split_axis=1, conca...  5.53 us
    all_to_all x1, starting transfers between devices, on_device(): lax.all_to_all(send_tokens, 'expert', split_axis=0, concat_axis=0, tiled=...  3.4 us
  transfers between devices with their start and end apart: 4, of which 3 were waited for; matrix products, arithmetic and copies ran while one was open for 4% of the time, Pallas kernels for 0%

commit v1 on v0

--- a/solution.py
+++ b/solution.py
@@ -89,8 +89,14 @@
     summed = lax.psum_scatter(
         (from_gate + from_up).astype(jnp.bfloat16), "dp", scatter_dimension=0, tiled=True
     ).astype(jnp.float32)
-    returned = lax.all_to_all(
-        summed.astype(jnp.bfloat16), "expert", split_axis=1, concat_axis=1, tiled=True
+    returned = jnp.concatenate(
+        lax.all_to_all(
+            jnp.stack(jnp.split(summed.astype(jnp.bfloat16), lax.axis_size("expert"), axis=1)),
+            "expert",
+            0,
+            0,
+        ),
+        axis=1,
     ).astype(summed.dtype)
     owner_match = (flat_source[:, None] == jnp.arange(row_count, dtype=jnp.int32)[None, :]).astype(
         jnp.float32

time: 117 us -> 125 us (1.068)
  local copies, waits for them, and re-layouts: 6.35 us -> 14.6 us
    unnamed x8 -> x22, local copies, waits for them, and re-layouts: 3.05 us -> 7.51 us
    split x0 -> x1, local copies, waits for them, and re-layouts: none -> 3.17 us  [on_device(): jnp.split(summed.astype(jnp.bfloat16), lax.axis_size('expert'), axis=1)]
where the time goes in v1:
time: 125 us; the launch traced here: 124 us
  waiting for transfers between devices  36.3 us (29%)
  blocking collectives  32.4 us (26%)
  between operations  14.9 us (12%)
  local copies, waits for them, and re-layouts  14.6 us (12%)
  starting transfers between devices  12.4 us (10%)
  matrix products  7.06 us (6%)
  other arithmetic  6.57 us (5%)
    unnamed x2, waiting for transfers between devices  24.5 us
    psum x1, blocking collectives, on_device(): forget_total = lax.psum(jnp.sum(forget_flags), 'expert')  13.7 us
    all_gather x1, blocking collectives, on_device(): lax.all_gather(part_tokens, 'dp', axis=1, tiled=True)  9.41 us
    all_gather x1, blocking collectives, on_device(): lax.all_gather(part_grads, 'dp', axis=1, tiled=True)  9.31 us
    unnamed x22, local copies, waits for them, and re-layouts  7.51 us
    all_to_all x1, waiting for transfers between devices, on_device(): lax.all_to_all(send_grads, 'expert', split_axis=0, concat_axis=0, tiled=T...  6.21 us
    all_to_all x1, waiting for transfers between devices, on_device(): lax.all_to_all(jnp.stack(jnp.split(summed.astype(jnp.bfloat16), lax.axis_...  5.55 us
    all_to_all x1, starting transfers between devices, on_device(): lax.all_to_all(jnp.stack(jnp.split(summed.astype(jnp.bfloat16), lax.axis_...  5.53 us
  transfers between devices with their start and end apart: 4, of which 3 were waited for; matrix products, arithmetic and copies ran while one was open for 4% of the time, Pallas kernels for 0%

profile of v1, /device:TPU:0, one launch (start us, length us, event | category | flops | bytes accessed | tf_op | source)
XLA Modules:
  0.0 124.2 jit_solution(10037323717572125247)
XLA Ops:
  7.2 0.9 fusion.16
  9.5 1.3 %reduce_sum.48 = s32[]{:T(128)} reduce(s32[256]{0:T(256)} %param.14, s32[]{:T(128)} %constant.4.clone.1), dimensions={0}, to_apply=%region_6.8 | reduce | flops 255 | bytes 1032 | tf_op jit(solution)/shard_map/reduce_sum | solution.py:47
  10.9 13.7 %psum.7 = s32[]{:T(128)} all-reduce(s32[]{:T(128)} %reduce_sum.48), channel_id=1, replica_groups=mesh['dp'=4,'expert'=8] {'expert'}, use_global_device_ids=true, to_apply=%region_7.9 | all-reduce | flops 1 | bytes 8 | tf_op jit(solution)/shard_map/psum | solution.py:47
  25.3 0.8 fusion.17
  26.1 0.7 compare_select_fusion.2
  27.0 1.1 concatenate.7
  28.1 0.9 gather_fusion.1
  29.0 0.8 multiply_convert_fusion
  29.9 3.4 %all-to-all-start.1 = ((bf16[8,16,896]{2,1,0:T(8,128)(2,1)}), bf16[8,16,896]{2,1,0:T(8,128)(2,1)S(1)}, u32[]{:S(2)}, u32[]{:S(2)}) async-start(bf16[8,16,896]{2,1,0:T(8,128)(2,1)} %bitcast.6), calls=%async_computation.1 | async-start | bytes 458752 | tf_op jit(solution)/shard_map/all_to_all | solution.py:64
  33.3 0.9 gather_fusion
  34.2 0.8 broadcast_select_fusion
  35.0 6.2 %all-to-all-done.1 = bf16[8,16,896]{2,1,0:T(8,128)(2,1)S(1)} async-done(((bf16[8,16,896]{2,1,0:T(8,128)(2,1)}), bf16[8,16,896]{2,1,0:T(8,128)(2,1)S(1)}, u32[]{:S(2)}, u32[]{:S(2)}) %all-to-all-start.1) | async-done | bytes 229408 | tf_op jit(solution)/shard_map/all_to_all | solution.py:64
  41.2 3.4 %all-to-all-start = ((bf16[8,16,896]{2,1,0:T(8,128)(2,1)}), bf16[8,16,896]{2,1,0:T(8,128)(2,1)S(1)}, u32[]{:S(2)}, u32[]{:S(2)}) async-start(bf16[8,16,896]{2,1,0:T(8,128)(2,1)} %bitcast.4), calls=%async_computation | async-start | bytes 458752 | tf_op jit(solution)/shard_map/all_to_all | solution.py:63
  44.7 9.3 %all_gather.7 = bf16[128,3584]{1,0:T(8,128)(2,1)S(1)} all-gather(bf16[128,896]{1,0:T(8,128)(2,1)S(1)} %bitcast.63), channel_id=1, replica_groups=mesh['dp'=4,'expert'=8] {'dp'}, dimensions={1}, use_global_device_ids=true | all-gather | bytes 1146880 | tf_op jit(solution)/shard_map/all_gather | solution.py:68
  54.0 9.4 %all_gather.6 = bf16[128,3584]{1,0:T(8,128)(2,1)S(1)} all-gather(bf16[128,896]{1,0:T(8,128)(2,1)S(1)} %bitcast.64), channel_id=1, replica_groups=mesh['dp'=4,'expert'=8] {'dp'}, dimensions={1}, use_global_device_ids=true | all-gather | bytes 1146880 | tf_op jit(solution)/shard_map/all_gather | solution.py:67
  63.8 1.6 %multiply_convert_fusion.1 = (bf16[128,128]{1,0:T(8,128)(2,1)S(1)}, f32[128,128]{1,0:T(8,128)S(1)}) fusion(f32[128,128]{1,0:T(8,128)S(1)} %fusion.8, bf16[128,3584]{1,0:T(8,128)(2,1)S(1)} %all_gather.7, bf16[1,128,3584]{2,1,0:T(8,128)(2,1)} %param.17), kind=kOutput, calls=%fused_computation.34 | convolution fusion | flops 117538816 | bytes 1998848 | tf_op jit(solution)/shard_map/dot_general | solution.py:76
  66.6 1.3 %copy.21 = bf16[3584,128]{1,0:T(8,128)(2,1)} copy(bf16[3584,128]{0,1:T(8,128)(2,1)S(1)} %fusion.3) | data formatting | bytes 1835008
  67.9 24.5 %reduce-scatter.4.cloned.1.call-done = bf16[896,128]{1,0:T(8,128)(2,1)} async-done(((bf16[3584,128]{1,0:T(8,128)(2,1)}), bf16[896,128]{1,0:T(8,128)(2,1)}) %reduce-scatter.4.cloned.1.call-update) | async-done | bytes 229392
  92.4 3.2 %fusion.19 = (bf16[896,16]{1,0:T(8,128)(2,1)S(1)}, bf16[896,16]{1,0:T(8,128)(2,1)S(1)}, bf16[896,16]{1,0:T(8,128)(2,1)S(1)}, bf16[896,16]{1,0:T(8,128)(2,1)S(1)}...) fusion(bf16[896,128]{1,0:T(8,128)(2,1)} %reduce-scatter.4.clone, ...), kind=kLoop, calls=%fused_computation.54 | loop fusion | bytes 458752 | tf_op jit(solution)/shard_map/split | solution.py:94
  95.6 1.0 copy.23
  96.6 0.6 bitcast_dynamic-update-slice_fusion.7
  98.1 0.6 bitcast_dynamic-update-slice_fusion.6
  98.8 0.6 bitcast_dynamic-update-slice_fusion.5
  99.4 0.6 bitcast_dynamic-update-slice_fusion.4
  100.0 0.6 bitcast_dynamic-update-slice_fusion.3
  100.6 0.6 bitcast_dynamic-update-slice_fusion.2
  101.8 0.6 bitcast_dynamic-update-slice_fusion
  102.4 5.5 %all-to-all-start.2 = ((bf16[8,896,16]{1,2,0:T(8,128)(2,1)}), bf16[8,896,16]{1,2,0:T(8,128)(2,1)S(1)}, u32[]{:S(2)}, u32[]{:S(2)}) async-start(bf16[8,896,16]{1,2,0:T(8,128)(2,1)} %bitcast_dynamic-update-slice_fusion), calls=%async_computation.2 | async-start | bytes 458752 | tf_op jit(solution)/shard_map/all_to_all | solution.py:93
  108.0 1.4 %fusion.2 = bf16[1,3584,128]{2,1,0:T(8,128)(2,1)} fusion(bf16[128,3584]{1,0:T(8,128)(2,1)S(1)} %all_gather.6, bf16[128,128]{1,0:T(8,128)(2,1)S(1)} %get-tuple-element.12), kind=kOutput, calls=%fused_computation.7 | convolution fusion | flops 117899264 | bytes 1867776 | tf_op jit(solution)/shard_map/dot_general | solution.py:84
  109.3 1.4 %fusion.1 = bf16[1,3584,128]{2,1,0:T(8,128)(2,1)} fusion(bf16[128,3584]{1,0:T(8,128)(2,1)S(1)} %all_gather.6, bf16[128,128]{1,0:T(8,128)(2,1)S(1)} %fusion.5), kind=kOutput, calls=%fused_computation.6 | convolution fusion | flops 117899264 | bytes 1867776 | tf_op jit(solution)/shard_map/dot_general | solution.py:81
  110.7 5.5 %all-to-all-done.2 = bf16[8,896,16]{1,2,0:T(8,128)(2,1)S(1)} async-done(((bf16[8,896,16]{1,2,0:T(8,128)(2,1)}), bf16[8,896,16]{1,2,0:T(8,128)(2,1)S(1)}, u32[]{:S(2)}, u32[]{:S(2)}) %all-to-all-start.2) | async-done | bytes 229408 | tf_op jit(solution)/shard_map/all_to_all | solution.py:93
  116.2 1.2 convolution_convert_fusion.2
  (39 shorter events, 4.9 us)
Async XLA Ops:
  7.2 56.2 %copy-start = (bf16[1,3584,128]{2,1,0:T(8,128)(2,1)S(1)}, bf16[1,3584,128]{2,1,0:T(8,128)(2,1)}, u32[]{:S(2)}) copy-start(bf16[1,3584,128]{2,1,0:T(8,128)(2,1)} %param.15) | copy-start | bytes 2752516
  27.0 6.2 %copy-start.2 = (bf16[256,896]{1,0:T(8,128)(2,1)S(1)}, bf16[256,896]{1,0:T(8,128)(2,1)}, u32[]{:S(2)}) copy-start(bf16[256,896]{1,0:T(8,128)(2,1)} %param.10) | copy-start | bytes 1376260
  29.9 11.3 %all-to-all-start.1 = ((bf16[8,16,896]{2,1,0:T(8,128)(2,1)}), bf16[8,16,896]{2,1,0:T(8,128)(2,1)S(1)}, u32[]{:S(2)}, u32[]{:S(2)}) async-start(bf16[8,16,896]{2,1,0:T(8,128)(2,1)} %bitcast.6), calls=%async_computation.1 | async-start | bytes 458752 | tf_op jit(solution)/shard_map/all_to_all | solution.py:64
  41.2 12.8 %all-to-all-start = ((bf16[8,16,896]{2,1,0:T(8,128)(2,1)}), bf16[8,16,896]{2,1,0:T(8,128)(2,1)S(1)}, u32[]{:S(2)}, u32[]{:S(2)}) async-start(bf16[8,16,896]{2,1,0:T(8,128)(2,1)} %bitcast.4), calls=%async_computation | async-start | bytes 458752 | tf_op jit(solution)/shard_map/all_to_all | solution.py:63
  44.6 47.8 %reduce-scatter.4.cloned.1.call-start = ((), (), s32[]{:S(2)}) async-start(), calls=%async_computation.4 | async-start | bytes 1146880
  63.4 2.0 %copy-start.1 = (bf16[1,3584,128]{2,1,0:T(8,128)(2,1)S(1)}, bf16[1,3584,128]{2,1,0:T(8,128)(2,1)}, u32[]{:S(2)}) copy-start(bf16[1,3584,128]{2,1,0:T(8,128)(2,1)} %param.16) | copy-start | bytes 2752516
  102.4 13.8 %all-to-all-start.2 = ((bf16[8,896,16]{1,2,0:T(8,128)(2,1)}), bf16[8,896,16]{1,2,0:T(8,128)(2,1)S(1)}, u32[]{:S(2)}, u32[]{:S(2)}) async-start(bf16[8,896,16]{1,2,0:T(8,128)(2,1)} %bitcast_dynamic-update-slice_fusion), calls=%async_computation.2 | async-start | bytes 458752 | tf_op jit(solution)/shard_map/all_to_all | solution.py:93
Sparse Core Ops, SparseCore 0:
  68.0 24.3 reduce-scatter.3
